TPU v7x, 512 devices: a whole 4x8x8 slice. The times are simulated.
512 devices in a mesh: depth: 16 (over x_hi, y), scan: 32 (over z, x_lo, core).
Axes of the slice: x: 4 (x_hi: 2, x_lo: 2; x = x_hi * 2 + x_lo), y: 8, z: 8, core: 2. Of those that a mesh axis runs over, the one named last changes fastest.
Arguments:
- object_slice: bfloat16 [2, 4, 512, 2048], P(None, None, 'depth', 'scan'), may hold values from -4 to 4
- probe_field: bfloat16 [2, 512, 512], replicated, may hold values from -2 to 2
- offsets: int32 [64, 2], replicated, may hold values from 0 to 1536
- assignment: int32 [64], P('scan'), may hold values from 0 to 63, each once
- intensities: float32 [64, 512, 512], P('scan', 'depth'), may hold values from 0 to 3
Outputs:
- object_grad: float32 [2, 4, 512, 2048], P(None, None, 'depth', 'scan')
- probe_grad: float32 [2, 512, 512], P(None, 'depth')
Inputs may be any that keep to these rules, and one draw needn't show every extreme that they name: `offsets`: each window lies inside the object window. `assignment`: every position stands in exactly one slot; slots s * 2 to s * 2 + 1 lie on index s of scan.
All inputs are finite; a program needn't handle non-finite values.
Results may differ from a plain program's by a relative error of at most 0.0003.
Values may be sent and summed in bfloat16 or wider, within the bound.
No kernel may reach another device: no remote copies, remote signals or barrier semaphores. Data moves between devices by JAX's collectives and lax.ppermute only.
A program may use at most 64 MiB of HBM per device.

v0:
```python
import math
import jax
import jax.numpy as jnp
from jax import lax
from jax.sharding import PartitionSpec as P

fresnel_scale = 4


def from_behind(block, axis, distance):
    devices = range(lax.axis_size(axis))
    route = [((i - distance) % len(devices), i) for i in devices]
    return lax.ppermute(block, axis, route)


def dft_table(size):
    index = jnp.arange(size, dtype=jnp.int32)
    turns = index[:, None] * index[None, :] % size
    angle = 2.0 * math.pi / size * turns.astype(jnp.float32)
    norm = 1.0 / math.sqrt(size)
    return (jnp.cos(angle) * norm, -jnp.sin(angle) * norm)


def chirp_phase(index, size):
    centred = index - size // 2
    period = 2 * fresnel_scale * size
    phase = centred * centred % period
    angle = math.pi / (fresnel_scale * size) * phase.astype(jnp.float32)
    return (jnp.cos(angle), jnp.sin(angle))


def contract(form, left_side, right_side):
    return jnp.einsum(
        form,
        left_side,
        right_side,
        precision=lax.Precision.HIGHEST,
        preferred_element_type=jnp.float32,
    )


def complex_mix(form, left_re, left_im, right_re, right_im):
    real_part = contract(form, left_re, right_re) - contract(form, left_im, right_im)
    imag_part = contract(form, left_re, right_im) + contract(form, left_im, right_re)
    return (real_part, imag_part)


def on_device(object_slice, probe_field, offsets, assignment, intensities):
    depth_count = lax.axis_size("depth")
    depth_index = lax.axis_index("depth")
    rows_dev = object_slice.shape[2]
    cycles = object_slice.shape[1]
    patch_side = probe_field.shape[2]
    pos_count = assignment.shape[0]
    total_pos = pos_count * lax.axis_size("scan")
    band_rows = lax.all_gather(object_slice, "scan", axis=3, tiled=True)
    full_width = band_rows.shape[3]
    flat_band = band_rows.reshape(2, cycles * rows_dev, full_width)
    position = offsets[assignment]
    top_row = position[:, 0]
    left_col = position[:, 1]
    table_re, table_im = dft_table(patch_side)
    row_ids = jnp.arange(rows_dev, dtype=jnp.int32)
    col_ids = jnp.arange(patch_side, dtype=jnp.int32)
    col_cos, col_sin = chirp_phase(col_ids, patch_side)
    zero_start = jnp.int32(0)

    def cut_tile(cycle_row, column):
        return lax.dynamic_slice(
            flat_band, (zero_start, cycle_row * rows_dev, column), (2, rows_dev, patch_side)
        )

    block_first = top_row // rows_dev
    offset_in = top_row % rows_dev
    first_block = block_first + (depth_index - block_first) % depth_count
    first_cycle = first_block // depth_count
    second_cycle = jnp.minimum(first_cycle + 1, cycles - 1)
    pair_tiles = jnp.stack(
        [jax.vmap(cut_tile)(first_cycle, left_col), jax.vmap(cut_tile)(second_cycle, left_col)], 1
    )
    levels = depth_count.bit_length() - 1
    amount = (depth_count - block_first % depth_count) % depth_count
    for level in range(levels):
        moved = from_behind(pair_tiles, "depth", 1 << level)
        taken = amount >> level & 1 == 1
        pair_tiles = jnp.where(taken[:, None, None, None, None], moved, pair_tiles)
    first_tile = pair_tiles[:, 0]
    outgoing = jnp.where(depth_index == 0, pair_tiles[:, 1], first_tile)
    following = from_behind(outgoing, "depth", depth_count - 1)
    stacked = jnp.concatenate([first_tile, following], 2)

    def take_rows(tile_pair, corner_row):
        return lax.dynamic_slice_in_dim(tile_pair, corner_row, rows_dev, 1)

    patch = jax.vmap(take_rows)(stacked, offset_in)
    patch_rows = jnp.broadcast_to(depth_index * rows_dev + row_ids[None, :], (pos_count, rows_dev))
    probe_rows = lax.dynamic_slice_in_dim(probe_field, depth_index * rows_dev, rows_dev, 1)[None]
    row_cos, row_sin = chirp_phase(patch_rows, patch_side)
    chirp_re = (
        row_cos[:, :, None] * col_cos[None, None, :] - row_sin[:, :, None] * col_sin[None, None, :]
    )
    chirp_im = (
        row_sin[:, :, None] * col_cos[None, None, :] + row_cos[:, :, None] * col_sin[None, None, :]
    )
    obj_re = patch[:, 0].astype(jnp.float32)
    obj_im = patch[:, 1].astype(jnp.float32)
    probe_re = probe_rows[:, 0].astype(jnp.float32)
    probe_im = probe_rows[:, 1].astype(jnp.float32)
    wave_re = probe_re * obj_re - probe_im * obj_im
    wave_im = probe_re * obj_im + probe_im * obj_re
    psi_re = wave_re * chirp_re - wave_im * chirp_im
    psi_im = wave_re * chirp_im + wave_im * chirp_re
    half_re, half_im = complex_mix("vk,pjk->pvj", table_re, table_im, psi_re, psi_im)
    half_re, half_im = (
        lax.all_to_all(half_re, "depth", split_axis=1, concat_axis=2, tiled=True),
        lax.all_to_all(half_im, "depth", split_axis=1, concat_axis=2, tiled=True),
    )
    far_re, far_im = complex_mix("pvj,ju->pvu", half_re, half_im, table_re, table_im)
    excess = far_re * far_re + far_im * far_im - intensities
    resid_re = excess * far_re
    resid_im = excess * far_im
    mid_re, mid_im = complex_mix("pvu,uj->pvj", resid_re, resid_im, table_re, -table_im)
    mid_re, mid_im = (
        lax.all_to_all(mid_re, "depth", split_axis=2, concat_axis=1, tiled=True),
        lax.all_to_all(mid_im, "depth", split_axis=2, concat_axis=1, tiled=True),
    )
    back_re, back_im = complex_mix("vk,pvj->pjk", table_re, -table_im, mid_re, mid_im)
    grad_re = back_re * chirp_re + back_im * chirp_im
    grad_im = back_im * chirp_re - back_re * chirp_im
    contrib = jnp.stack(
        [probe_re * grad_re + probe_im * grad_im, probe_re * grad_im - probe_im * grad_re], 1
    )
    term_re = obj_re * grad_re + obj_im * grad_im
    term_im = obj_re * grad_im - obj_im * grad_re
    grad_band = jnp.zeros((2, cycles * rows_dev, full_width), jnp.float32)

    def add_tile(band_now, tile_value, cycle_row, column):
        corner = (zero_start, cycle_row * rows_dev, column)
        current = lax.dynamic_slice(band_now, corner, (2, rows_dev, patch_side))
        return lax.dynamic_update_slice(band_now, current + tile_value, corner)

    empty_window = jnp.zeros((pos_count, 2, 2 * rows_dev, patch_side), jnp.float32)

    def place_rows(window_zero, tile_rows, corner_row):
        return lax.dynamic_update_slice_in_dim(window_zero, tile_rows, corner_row, 1)

    placed = jax.vmap(place_rows)(empty_window, contrib, offset_in)
    head_part = placed[:, :, :rows_dev]
    tail_part = placed[:, :, rows_dev:]
    returned = from_behind(tail_part, "depth", 1)
    is_first = depth_index == 0
    head_part = jnp.where(is_first, head_part, head_part + returned)
    second_part = jnp.where(is_first, returned, jnp.zeros_like(returned))
    grad_pair = jnp.stack([head_part, second_part], 1)
    amount_back = block_first % depth_count
    for level in range(levels):
        moved_back = from_behind(grad_pair, "depth", 1 << level)
        taken_back = amount_back >> level & 1 == 1
        grad_pair = jnp.where(taken_back[:, None, None, None, None], moved_back, grad_pair)
    for slot_index in range(pos_count):
        grad_band = add_tile(
            grad_band, grad_pair[slot_index, 0], first_cycle[slot_index], left_col[slot_index]
        )
        grad_band = add_tile(
            grad_band, grad_pair[slot_index, 1], second_cycle[slot_index], left_col[slot_index]
        )
    probe_sum = jnp.stack([jnp.sum(term_re, 0), jnp.sum(term_im, 0)])
    probe_grad = lax.psum(probe_sum, "scan")
    object_grad = lax.psum_scatter(
        grad_band.reshape(2, cycles, rows_dev, full_width), "scan", scatter_dimension=3, tiled=True
    )
    return (object_grad, probe_grad * total_pos ** (-0.5))


def solution(mesh):
    return jax.shard_map(
        on_device,
        mesh=mesh,
        in_specs=(P(None, None, "depth", "scan"), P(), P(), P("scan"), P("scan", "depth", None)),
        out_specs=(P(None, None, "depth", "scan"), P(None, "depth", None)),
        check_vma=False,
    )
```

profile of v0, /device:TPU:8, one launch (start us, length us, event | category | flops | bytes accessed | tf_op | source)
XLA Modules:
  0.0 748.6 jit_solution(7698439106445803496)
XLA Ops:
  7.2 1.7 copy.63
  11.9 73.0 %all-gather.2.cloned.1.call-done = bf16[2,4,32,2048]{2,1,0,3:T(4,128)(2,1)} async-done(((bf16[2,4,32,64]{2,1,0,3:T(4,128)(2,1)}), bf16[2,4,32,2048]{2,1,0,3:T(4,128)(2,1)}) %all-gather.2.cloned.1.call-update) | async-done | bytes 1048592 | tf_op jit(solution)/shard_map/all_gather | solution.py:56
  85.0 5.5 copy.64
  90.5 4.2 while.4
  91.2 1.4 dynamic-slice_bitcast_fusion.6
  93.3 1.4 dynamic-slice_bitcast_fusion.6
  94.8 4.2 while.3
  95.4 1.4 dynamic-slice_bitcast_fusion.5
  97.5 1.4 dynamic-slice_bitcast_fusion.5
  99.4 3.4 collective-permute-start
  102.9 6.9 collective-permute-done
  110.3 4.5 collective-permute-start.1
  114.8 9.8 %collective-permute-done.1 = bf16[2,2,2,32,512]{4,2,0,3,1:T(2,128)(2,1)S(1)} collective-permute-done((bf16[2,2,2,32,512]{4,2,0,3,1:T(2,128)(2,1)S(1)}, bf16[2,2,2,32,512]{4,2,0,3,1:T(2,128)(2,1)S(1)}, u32[]{:S(2)}, u32[]{:S(2)}) %collective-permute-start.1) | collective-permute-done | bytes 262176 | tf_op jit(solution)/shard_map/ppermute | solution.py:13
  125.3 4.8 collective-permute-start.2
  130.1 15.7 %collective-permute-done.2 = bf16[2,2,2,32,512]{4,2,0,3,1:T(2,128)(2,1)S(1)} collective-permute-done((bf16[2,2,2,32,512]{4,2,0,3,1:T(2,128)(2,1)S(1)}, bf16[2,2,2,32,512]{4,2,0,3,1:T(2,128)(2,1)S(1)}, u32[]{:S(2)}, u32[]{:S(2)}) %collective-permute-start.2) | collective-permute-done | bytes 262176 | tf_op jit(solution)/shard_map/ppermute | solution.py:13
  146.2 2.8 collective-permute-start.3
  149.0 8.0 %collective-permute-done.3 = bf16[2,2,2,32,512]{4,2,0,3,1:T(2,128)(2,1)S(1)} collective-permute-done((bf16[2,2,2,32,512]{4,2,0,3,1:T(2,128)(2,1)S(1)}, bf16[2,2,2,32,512]{4,2,0,3,1:T(2,128)(2,1)S(1)}, u32[]{:S(2)}, u32[]{:S(2)}) %collective-permute-start.3) | collective-permute-done | bytes 262176 | tf_op jit(solution)/shard_map/ppermute | solution.py:13
  157.6 8.7 %collective-permute-start.4 = (bf16[2,2,32,512]{3,1,0,2:T(2,128)(2,1)S(1)}, bf16[2,2,32,512]{3,1,0,2:T(2,128)(2,1)S(1)}, u32[]{:S(2)}, u32[]{:S(2)}) collective-permute-start(bf16[2,2,32,512]{3,1,0,2:T(2,128)(2,1)S(1)} %broadcast_select_fusion.8), channel_id=1, source_target_pairs={{32,0},{64,32},{96,64},{128,96},{160,128},{192,160},{224,192},{256... | collective-permute-start | bytes 393224 | tf_op jit(solution)/shard_map/ppermute | solution.py:13
  166.4 2.2 collective-permute-done.4
  170.0 5.0 fusion.27
  175.0 5.0 fusion.23
  180.0 5.2 fusion.1
  186.7 7.4 all-to-all-start
  194.0 5.0 fusion
  200.5 3.1 all-to-all-done
  203.5 7.1 all-to-all-start.1
  213.1 4.8 fusion.25
  217.8 4.8 fusion.10
  224.6 4.7 convolution_add_fusion.2
  229.3 4.9 convolution_subtract_fusion.2
  234.3 4.8 fusion.7
  239.1 4.8 fusion.20
  243.9 4.8 convolution_subtract_fusion.1
  250.2 9.6 %all-to-all-start.2 = ((f32[16,1,2048]{2,1,0:T(1,128)}), f32[16,1,2048]{2,1,0:T(1,128)S(1)}, u32[]{:S(2)}, u32[]{:S(2)}) async-start(f32[16,1,2048]{2,1,0:T(1,128)} %reshape.375), calls=%async_computation.2 | async-start | bytes 262144 | tf_op jit(solution)/shard_map/all_to_all | solution.py:124
  259.8 4.7 convolution_add_fusion.1
  266.0 3.3 all-to-all-done.2
  269.3 6.3 all-to-all-start.3
  277.7 5.0 fusion.18
  282.7 2.5 all-to-all-done.3
  287.1 4.8 fusion.15
  291.9 4.8 convolution_add_fusion
  296.7 4.9 fusion.40
  301.8 14.5 %while.5 = (s32[]{:T(128)}, f32[2,2,64,512]{3,1,0,2:T(2,128)S(1)}, s32[2,4]{1,0:T(2,128)S(1)}, f32[2,2,32,512]{3,2,0,1:T(8,128)S(1)}, s32[]{:T(128)}, /*index=5*/s32[4]{0:T(128)S(1)}) while((s32[]{:T(128)}, f32[2,2,64,512]{3,1,0,2:T(2,128)S(1)}, s32[2,4]{1,0:T(2,128)S(1)}, f32[2,2,32,512]{3,2,0,1:T(8,128)S(1)}, s32[]{:T(128)}, ...), condition=%wide.while_cond.2, body=%wide.while_body.2.sunk | while | flops 32797 | bytes 917703 | solution.py:145
  302.5 3.2 and_reduce_fusion.2
  309.7 3.2 and_reduce_fusion.2
  316.3 2.6 collective-permute-start.5
  318.9 5.6 collective-permute-done.5
  325.0 4.3 collective-permute-start.6
  329.3 9.1 %collective-permute-done.6 = f32[2,2,2,32,512]{4,2,0,3,1:T(2,128)S(1)} collective-permute-done((f32[2,2,2,32,512]{4,2,0,3,1:T(2,128)S(1)}, f32[2,2,2,32,512]{4,2,0,3,1:T(2,128)S(1)}, u32[]{:S(2)}, u32[]{:S(2)}) %collective-permute-start.6) | collective-permute-done | bytes 524320 | tf_op jit(solution)/shard_map/ppermute | solution.py:13
  338.8 4.0 collective-permute-start.7
  342.8 18.4 %collective-permute-done.7 = f32[2,2,2,32,512]{4,2,0,3,1:T(2,128)S(1)} collective-permute-done((f32[2,2,2,32,512]{4,2,0,3,1:T(2,128)S(1)}, f32[2,2,2,32,512]{4,2,0,3,1:T(2,128)S(1)}, u32[]{:S(2)}, u32[]{:S(2)}) %collective-permute-start.7) | collective-permute-done | bytes 524320 | tf_op jit(solution)/shard_map/ppermute | solution.py:13
  361.6 4.7 collective-permute-start.8
  366.3 20.3 %collective-permute-done.8 = f32[2,2,2,32,512]{4,2,0,3,1:T(2,128)S(1)} collective-permute-done((f32[2,2,2,32,512]{4,2,0,3,1:T(2,128)S(1)}, f32[2,2,2,32,512]{4,2,0,3,1:T(2,128)S(1)}, u32[]{:S(2)}, u32[]{:S(2)}) %collective-permute-start.8) | collective-permute-done | bytes 524320 | tf_op jit(solution)/shard_map/ppermute | solution.py:13
  387.0 1.9 collective-permute-start.9
  397.3 2.3 collective-permute-done.9
  401.8 6.2 dynamic_update_slice.12
  409.1 6.2 dynamic_update_slice.13
  416.4 6.1 dynamic_update_slice.14
  423.7 6.1 dynamic_update_slice.15
  429.8 6.1 copy.84
  436.0 8.6 %reshape.365 = f32[2048,256]{1,0:T(8,128)} reshape(f32[2048,2,4,32]{3,2,1,0:T(4,128)} %bitcast.195) | data formatting | bytes 4194304
  444.6 169.5 %all-reduce.2.cloned.1.call-done = f32[2,32,512]{2,1,0:T(8,128)} async-done(((f32[2,32,512]{2,1,0:T(8,128)}), f32[2,32,512]{2,1,0:T(8,128)}) %all-reduce.2.cloned.1.call-update) | async-done | bytes 131088 | tf_op jit(solution)/shard_map/psum | solution.py:168
  614.0 1.6 broadcast_multiply_fusion
  615.6 124.2 %reduce-scatter.4.cloned.1.call-done = f32[64,256]{1,0:T(8,128)} async-done(((f32[2048,256]{1,0:T(8,128)}), f32[64,256]{1,0:T(8,128)}) %reduce-scatter.4.cloned.1.call-update) | async-done | bytes 65552
  (115 shorter events, 42.9 us)
Async XLA Ops:
  7.2 107.7 %copy-start = (bf16[2,512,512]{2,1,0:T(8,128)(2,1)S(1)}, bf16[2,512,512]{2,1,0:T(8,128)(2,1)}, u32[]{:S(2)}) copy-start(bf16[2,512,512]{2,1,0:T(8,128)(2,1)} %param.6) | copy-start | bytes 3145732
  7.2 77.8 %all-gather.2.cloned.1.call-start = ((), (), s32[]{:S(2)}) async-start(), calls=%async_computation.5 | async-start | bytes 4325376 | tf_op jit(solution)/shard_map/all_gather | solution.py:56
  99.4 10.3 %collective-permute-start = (bf16[2,2,2,32,512]{4,2,0,3,1:T(2,128)(2,1)S(1)}, bf16[2,2,2,32,512]{4,2,0,3,1:T(2,128)(2,1)S(1)}, u32[]{:S(2)}, u32[]{:S(2)}) collective-permute-start(bf16[2,2,2,32,512]{4,2,0,3,1:T(2,128)(2,1)S(1)} %pad_maximum_fusion.1), channel_id=1, source_target_pairs={{480,0},{0,32},{32,64},{64,96},{96,128},{128,160},{160,192},{192,2... | collective-permute-start | bytes 786440 | tf_op jit(solution)/shard_map/ppermute | solution.py:13
  110.3 14.4 %collective-permute-start.1 = (bf16[2,2,2,32,512]{4,2,0,3,1:T(2,128)(2,1)S(1)}, bf16[2,2,2,32,512]{4,2,0,3,1:T(2,128)(2,1)S(1)}, u32[]{:S(2)}, u32[]{:S(2)}) collective-permute-start(bf16[2,2,2,32,512]{4,2,0,3,1:T(2,128)(2,1)S(1)} %broadcast_select_fusion.4), channel_id=1, source_target_pairs={{448,0},{480,32},{0,64},{32,96},{64,128},{96,160},{128,192},{160,2... | collective-permute-start | bytes 786440 | tf_op jit(solution)/shard_map/ppermute | solution.py:13
  125.3 20.5 %collective-permute-start.2 = (bf16[2,2,2,32,512]{4,2,0,3,1:T(2,128)(2,1)S(1)}, bf16[2,2,2,32,512]{4,2,0,3,1:T(2,128)(2,1)S(1)}, u32[]{:S(2)}, u32[]{:S(2)}) collective-permute-start(bf16[2,2,2,32,512]{4,2,0,3,1:T(2,128)(2,1)S(1)} %broadcast_select_fusion.5), channel_id=1, source_target_pairs={{384,0},{416,32},{448,64},{480,96},{0,128},{32,160},{64,192},{96,2... | collective-permute-start | bytes 786440 | tf_op jit(solution)/shard_map/ppermute | solution.py:13
  146.2 10.9 %collective-permute-start.3 = (bf16[2,2,2,32,512]{4,2,0,3,1:T(2,128)(2,1)S(1)}, bf16[2,2,2,32,512]{4,2,0,3,1:T(2,128)(2,1)S(1)}, u32[]{:S(2)}, u32[]{:S(2)}) collective-permute-start(bf16[2,2,2,32,512]{4,2,0,3,1:T(2,128)(2,1)S(1)} %broadcast_select_fusion.6), channel_id=1, source_target_pairs={{256,0},{288,32},{320,64},{352,96},{384,128},{416,160},{448,192},{... | collective-permute-start | bytes 786440 | tf_op jit(solution)/shard_map/ppermute | solution.py:13
  157.6 11.0 %collective-permute-start.4 = (bf16[2,2,32,512]{3,1,0,2:T(2,128)(2,1)S(1)}, bf16[2,2,32,512]{3,1,0,2:T(2,128)(2,1)S(1)}, u32[]{:S(2)}, u32[]{:S(2)}) collective-permute-start(bf16[2,2,32,512]{3,1,0,2:T(2,128)(2,1)S(1)} %broadcast_select_fusion.8), channel_id=1, source_target_pairs={{32,0},{64,32},{96,64},{128,96},{160,128},{192,160},{224,192},{256... | collective-permute-start | bytes 393224 | tf_op jit(solution)/shard_map/ppermute | solution.py:13
  186.7 16.9 %all-to-all-start = ((f32[16,1,2048]{2,1,0:T(1,128)}), f32[16,1,2048]{2,1,0:T(1,128)S(1)}, u32[]{:S(2)}, u32[]{:S(2)}) async-start(f32[16,1,2048]{2,1,0:T(1,128)} %reshape.369), calls=%async_computation | async-start | bytes 262144 | tf_op jit(solution)/shard_map/all_to_all | solution.py:115
  203.5 19.1 %all-to-all-start.1 = ((f32[16,1,2048]{2,1,0:T(1,128)}), f32[16,1,2048]{2,1,0:T(1,128)S(1)}, u32[]{:S(2)}, u32[]{:S(2)}) async-start(f32[16,1,2048]{2,1,0:T(1,128)} %reshape.371), calls=%async_computation.1 | async-start | bytes 262144 | tf_op jit(solution)/shard_map/all_to_all | solution.py:116
  229.3 5.0 copy-start.3
  250.2 19.1 %all-to-all-start.2 = ((f32[16,1,2048]{2,1,0:T(1,128)}), f32[16,1,2048]{2,1,0:T(1,128)S(1)}, u32[]{:S(2)}, u32[]{:S(2)}) async-start(f32[16,1,2048]{2,1,0:T(1,128)} %reshape.375), calls=%async_computation.2 | async-start | bytes 262144 | tf_op jit(solution)/shard_map/all_to_all | solution.py:124
  269.3 15.8 %all-to-all-start.3 = ((f32[16,1,2048]{2,1,0:T(1,128)}), f32[16,1,2048]{2,1,0:T(1,128)S(1)}, u32[]{:S(2)}, u32[]{:S(2)}) async-start(f32[16,1,2048]{2,1,0:T(1,128)} %reshape.373), calls=%async_computation.3 | async-start | bytes 262144 | tf_op jit(solution)/shard_map/all_to_all | solution.py:125
  275.6 338.4 %all-reduce.2.cloned.1.call-start = ((), (), s32[]{:S(2)}) async-start(), calls=%async_computation.6 | async-start | bytes 262144 | tf_op jit(solution)/shard_map/psum | solution.py:168
  296.6 5.1 copy-start.2
  316.3 8.3 %collective-permute-start.5 = (f32[2,2,32,512]{3,1,0,2:T(2,128)S(1)}, f32[2,2,32,512]{3,1,0,2:T(2,128)S(1)}, u32[]{:S(2)}, u32[]{:S(2)}) collective-permute-start(f32[2,2,32,512]{3,1,0,2:T(2,128)S(1)} %slice.75), channel_id=1, source_target_pairs={{480,0},{0,32},{32,64},{64,96},{96,128},{128,160},{160,192},{192,2... | collective-permute-start | bytes 786440 | tf_op jit(solution)/shard_map/ppermute | solution.py:13
  325.0 13.3 %collective-permute-start.6 = (f32[2,2,2,32,512]{4,2,0,3,1:T(2,128)S(1)}, f32[2,2,2,32,512]{4,2,0,3,1:T(2,128)S(1)}, u32[]{:S(2)}, u32[]{:S(2)}) collective-permute-start(f32[2,2,2,32,512]{4,2,0,3,1:T(2,128)S(1)} %pad_maximum_fusion), channel_id=1, source_target_pairs={{480,0},{0,32},{32,64},{64,96},{96,128},{128,160},{160,192},{192,2... | collective-permute-start | bytes 1572872 | tf_op jit(solution)/shard_map/ppermute | solution.py:13
  338.8 22.4 %collective-permute-start.7 = (f32[2,2,2,32,512]{4,2,0,3,1:T(2,128)S(1)}, f32[2,2,2,32,512]{4,2,0,3,1:T(2,128)S(1)}, u32[]{:S(2)}, u32[]{:S(2)}) collective-permute-start(f32[2,2,2,32,512]{4,2,0,3,1:T(2,128)S(1)} %broadcast_select_fusion), channel_id=1, source_target_pairs={{448,0},{480,32},{0,64},{32,96},{64,128},{96,160},{128,192},{160,2... | collective-permute-start | bytes 1572872 | tf_op jit(solution)/shard_map/ppermute | solution.py:13
  361.6 25.0 %collective-permute-start.8 = (f32[2,2,2,32,512]{4,2,0,3,1:T(2,128)S(1)}, f32[2,2,2,32,512]{4,2,0,3,1:T(2,128)S(1)}, u32[]{:S(2)}, u32[]{:S(2)}) collective-permute-start(f32[2,2,2,32,512]{4,2,0,3,1:T(2,128)S(1)} %broadcast_select_fusion.1), channel_id=1, source_target_pairs={{384,0},{416,32},{448,64},{480,96},{0,128},{32,160},{64,192},{96,2... | collective-permute-start | bytes 1572872 | tf_op jit(solution)/shard_map/ppermute | solution.py:13
  387.0 12.6 %collective-permute-start.9 = (f32[2,2,2,32,512]{4,2,0,3,1:T(2,128)S(1)}, f32[2,2,2,32,512]{4,2,0,3,1:T(2,128)S(1)}, u32[]{:S(2)}, u32[]{:S(2)}) collective-permute-start(f32[2,2,2,32,512]{4,2,0,3,1:T(2,128)S(1)} %broadcast_select_fusion.2), channel_id=1, source_target_pairs={{256,0},{288,32},{320,64},{352,96},{384,128},{416,160},{448,192},{... | collective-permute-start | bytes 1572872 | tf_op jit(solution)/shard_map/ppermute | solution.py:13
  397.2 342.6 %reduce-scatter.4.cloned.1.call-start = ((), (), s32[]{:S(2)}) async-start(), calls=%async_computation.7 | async-start | bytes 2162688
  399.9 0.8 copy-start.1
Sparse Core Ops, SparseCore 0:
  10.7 74.1 all-gather.1
  397.4 216.6 all-reduce.1
  616.8 122.9 reduce-scatter.3
where the time goes:
time: 754 us; the launch traced here: 749 us
  waiting for transfers between devices  474 us (63%)
  local copies, waits for them, and re-layouts  79.3 us (11%)
  matrix products  78 us (10%)
  starting transfers between devices  72.2 us (10%)
  other arithmetic  23.6 us (3%)
  between operations  21.3 us (3%)
    psum x1, waiting for transfers between devices, on_device(): probe_grad = lax.psum(probe_sum, 'scan')  169 us
    unnamed x4, waiting for transfers between devices  124 us
    ppermute x10, waiting for transfers between devices, from_behind(): return lax.ppermute(block, axis, route)  98.4 us
    dot_general x16, matrix products, contract(): jnp.einsum(form, left_side, right_side, precision=lax.Precision.HIGHEST,...  78 us
    all_gather x1, waiting for transfers between devices, on_device(): band_rows = lax.all_gather(object_slice, 'scan', axis=3, tiled=True)  73 us
    ppermute x10, starting transfers between devices, from_behind(): return lax.ppermute(block, axis, route)  41.7 us
    unnamed x26, local copies, waits for them, and re-layouts  26.5 us
    dynamic_update_slice x4, local copies, waits for them, and re-layouts, add_tile(): return lax.dynamic_update_slice(band_now, current + tile_value, corner)  24.7 us
  transfers between devices with their start and end apart: 17, of which 16 were waited for; matrix products, arithmetic and copies ran while one was open for 11% of the time, Pallas kernels for 0%

commit v1 on v0

--- a/solution.py
+++ b/solution.py
@@ -3,8 +3,15 @@
 import jax.numpy as jnp
 from jax import lax
 from jax.sharding import PartitionSpec as P
+from jax.lax import all_to_all, axis_size
 
 fresnel_scale = 4
+
+
+def try_all_vector(dev_axis, here_x, dim_i):
+    parts_out = jnp.stack([here_x for _ in range(axis_size(dev_axis))], axis=0)
+    lower = all_to_all(parts_out, dev_axis, 0, 0)
+    return jnp.concatenate(lower, axis=dim_i)
 
 
 def from_behind(block, axis, distance):
@@ -53,7 +60,7 @@
     patch_side = probe_field.shape[2]
     pos_count = assignment.shape[0]
     total_pos = pos_count * lax.axis_size("scan")
-    band_rows = lax.all_gather(object_slice, "scan", axis=3, tiled=True)
+    band_rows = try_all_vector("scan", object_slice, 3)
     full_width = band_rows.shape[3]
     flat_band = band_rows.reshape(2, cycles * rows_dev, full_width)
     position = offsets[assignment]

time: 754 us -> 726 us (0.963)
  waiting for transfers between devices: 474 us -> 424 us
  starting transfers between devices: 72.2 us -> 86.1 us
    all_gather x1 -> x0, waiting for transfers between devices: 73 us -> none  [on_device(): band_rows = lax.all_gather(object_slice, 'scan', axis=3, tiled=True)]
    all_to_all x0 -> x1, waiting for transfers between devices: none -> 27.5 us  [try_all_vector(): lower = all_to_all(parts_out, dev_axis, 0, 0)]
    all_to_all x0 -> x1, starting transfers between devices: none -> 11.8 us  [try_all_vector(): lower = all_to_all(parts_out, dev_axis, 0, 0)]
    unnamed x26 -> x33, local copies, waits for them, and re-layouts: 26.5 us -> 30.2 us
    unnamed x4 -> x3, waiting for transfers between devices: 124 us -> 124 us
where the time goes in v1:
time: 726 us; the launch traced here: 718 us
  waiting for transfers between devices  424 us (58%)
  starting transfers between devices  86.1 us (12%)
  local copies, waits for them, and re-layouts  85.2 us (12%)
  matrix products  78 us (11%)
  other arithmetic  22.3 us (3%)
  between operations  21.6 us (3%)
    psum x1, waiting for transfers between devices, on_device(): probe_grad = lax.psum(probe_sum, 'scan')  169 us
    unnamed x3, waiting for transfers between devices  124 us
    ppermute x10, waiting for transfers between devices, from_behind(): return lax.ppermute(block, axis, route)  94.9 us
    dot_general x16, matrix products, contract(): jnp.einsum(form, left_side, right_side, precision=lax.Precision.HIGHEST,...  78 us
    ppermute x10, starting transfers between devices, from_behind(): return lax.ppermute(block, axis, route)  43.9 us
    unnamed x33, local copies, waits for them, and re-layouts  30.2 us
    all_to_all x1, waiting for transfers between devices, try_all_vector(): lower = all_to_all(parts_out, dev_axis, 0, 0)  27.5 us
    dynamic_update_slice x4, local copies, waits for them, and re-layouts, add_tile(): return lax.dynamic_update_slice(band_now, current + tile_value, corner)  24.7 us
  transfers between devices with their start and end apart: 17, of which 16 were waited for; matrix products, arithmetic and copies ran while one was open for 11% of the time, Pallas kernels for 0%

profile of v1, /device:TPU:8, one launch (start us, length us, event | category | flops | bytes accessed | tf_op | source)
XLA Modules:
  0.0 717.8 jit_solution(3329571264122866601)
XLA Ops:
  7.2 1.4 stack.26
  8.6 2.3 reshape.371
  10.9 11.8 %all-to-all-start = ((bf16[32,2,8192]{2,1,0:T(2,128)(2,1)}), bf16[32,2,8192]{2,1,0:T(2,128)(2,1)}, u32[]{:S(2)}, u32[]{:S(2)}) async-start(bf16[32,2,8192]{2,1,0:T(2,128)(2,1)} %reshape.371), calls=%async_computation | async-start | bytes 2097152 | tf_op jit(solution)/shard_map/all_to_all | solution.py:13
  23.7 27.5 %all-to-all-done = bf16[32,2,8192]{2,1,0:T(2,128)(2,1)} async-done(((bf16[32,2,8192]{2,1,0:T(2,128)(2,1)}), bf16[32,2,8192]{2,1,0:T(2,128)(2,1)}, u32[]{:S(2)}, u32[]{:S(2)}) %all-to-all-start) | async-done | bytes 1048608 | tf_op jit(solution)/shard_map/all_to_all | solution.py:13
  51.2 3.8 reshape.372
  55.0 2.7 copy.60
  57.7 3.4 reshape_reshape.3
  61.2 4.2 while.4
  65.5 4.3 while.3
  66.2 1.4 dynamic-slice_bitcast_fusion.5
  70.2 3.5 collective-permute-start
  73.7 6.3 collective-permute-done
  80.5 4.8 collective-permute-start.1
  85.4 9.0 %collective-permute-done.1 = bf16[2,2,2,32,512]{4,2,0,3,1:T(2,128)(2,1)S(1)} collective-permute-done((bf16[2,2,2,32,512]{4,2,0,3,1:T(2,128)(2,1)S(1)}, bf16[2,2,2,32,512]{4,2,0,3,1:T(2,128)(2,1)S(1)}, u32[]{:S(2)}, u32[]{:S(2)}) %collective-permute-start.1) | collective-permute-done | bytes 262176 | tf_op jit(solution)/shard_map/ppermute | solution.py:20
  95.0 5.0 collective-permute-start.2
  100.1 14.7 %collective-permute-done.2 = bf16[2,2,2,32,512]{4,2,0,3,1:T(2,128)(2,1)S(1)} collective-permute-done((bf16[2,2,2,32,512]{4,2,0,3,1:T(2,128)(2,1)S(1)}, bf16[2,2,2,32,512]{4,2,0,3,1:T(2,128)(2,1)S(1)}, u32[]{:S(2)}, u32[]{:S(2)}) %collective-permute-start.2) | collective-permute-done | bytes 262176 | tf_op jit(solution)/shard_map/ppermute | solution.py:20
  115.1 3.6 collective-permute-start.3
  118.8 6.4 collective-permute-done.3
  125.7 11.2 %collective-permute-start.4 = (bf16[2,2,32,512]{3,1,0,2:T(2,128)(2,1)S(1)}, bf16[2,2,32,512]{3,1,0,2:T(2,128)(2,1)S(1)}, u32[]{:S(2)}, u32[]{:S(2)}) collective-permute-start(bf16[2,2,32,512]{3,1,0,2:T(2,128)(2,1)S(1)} %broadcast_select_fusion.8), channel_id=1, source_target_pairs={{32,0},{64,32},{96,64},{128,96},{160,128},{192,160},{224,192},{256... | collective-permute-start | bytes 393224 | tf_op jit(solution)/shard_map/ppermute | solution.py:20
  137.1 2.2 collective-permute-done.4
  140.7 5.0 fusion.27
  145.7 5.0 fusion.23
  150.7 5.2 fusion.1
  157.3 7.4 %all-to-all-start.1 = ((f32[16,1,2048]{2,1,0:T(1,128)}), f32[16,1,2048]{2,1,0:T(1,128)S(1)}, u32[]{:S(2)}, u32[]{:S(2)}) async-start(f32[16,1,2048]{2,1,0:T(1,128)} %reshape.373), calls=%async_computation.1 | async-start | bytes 262144 | tf_op jit(solution)/shard_map/all_to_all | solution.py:122
  164.7 5.0 fusion
  171.2 3.1 all-to-all-done.1
  174.2 7.1 all-to-all-start.2
  183.8 4.8 fusion.25
  188.6 4.8 fusion.10
  195.3 4.7 convolution_add_fusion.2
  200.1 5.0 convolution_subtract_fusion.2
  205.0 4.8 fusion.7
  209.9 4.8 fusion.20
  214.7 4.8 convolution_subtract_fusion.1
  220.9 9.6 %all-to-all-start.3 = ((f32[16,1,2048]{2,1,0:T(1,128)}), f32[16,1,2048]{2,1,0:T(1,128)S(1)}, u32[]{:S(2)}, u32[]{:S(2)}) async-start(f32[16,1,2048]{2,1,0:T(1,128)} %reshape.379), calls=%async_computation.3 | async-start | bytes 262144 | tf_op jit(solution)/shard_map/all_to_all | solution.py:131
  230.5 4.7 convolution_add_fusion.1
  236.7 3.3 all-to-all-done.3
  240.1 6.3 all-to-all-start.4
  248.4 5.0 fusion.18
  253.4 2.5 all-to-all-done.4
  257.8 4.8 fusion.15
  262.6 4.8 convolution_add_fusion
  267.4 4.9 fusion.40
  272.5 14.5 %while.5 = (s32[]{:T(128)}, f32[2,2,64,512]{3,1,0,2:T(2,128)S(1)}, s32[2,4]{1,0:T(2,128)S(1)}, f32[2,2,32,512]{3,2,0,1:T(8,128)S(1)}, s32[]{:T(128)}, /*index=5*/s32[4]{0:T(128)S(1)}) while((s32[]{:T(128)}, f32[2,2,64,512]{3,1,0,2:T(2,128)S(1)}, s32[2,4]{1,0:T(2,128)S(1)}, f32[2,2,32,512]{3,2,0,1:T(8,128)S(1)}, s32[]{:T(128)}, ...), condition=%wide.while_cond.2, body=%wide.while_body.2.sunk | while | flops 32797 | bytes 917703 | solution.py:152
  273.2 3.3 and_reduce_fusion.2
  280.5 3.3 and_reduce_fusion.2
  287.0 2.6 collective-permute-start.5
  289.7 5.6 collective-permute-done.5
  295.8 3.9 collective-permute-start.6
  299.7 9.4 %collective-permute-done.6 = f32[2,2,2,32,512]{4,2,0,3,1:T(2,128)S(1)} collective-permute-done((f32[2,2,2,32,512]{4,2,0,3,1:T(2,128)S(1)}, f32[2,2,2,32,512]{4,2,0,3,1:T(2,128)S(1)}, u32[]{:S(2)}, u32[]{:S(2)}) %collective-permute-start.6) | collective-permute-done | bytes 524320 | tf_op jit(solution)/shard_map/ppermute | solution.py:20
  309.5 2.9 collective-permute-start.7
  312.4 21.0 %collective-permute-done.7 = f32[2,2,2,32,512]{4,2,0,3,1:T(2,128)S(1)} collective-permute-done((f32[2,2,2,32,512]{4,2,0,3,1:T(2,128)S(1)}, f32[2,2,2,32,512]{4,2,0,3,1:T(2,128)S(1)}, u32[]{:S(2)}, u32[]{:S(2)}) %collective-permute-start.7) | collective-permute-done | bytes 524320 | tf_op jit(solution)/shard_map/ppermute | solution.py:20
  334.0 3.1 collective-permute-start.8
  337.1 19.0 %collective-permute-done.8 = f32[2,2,2,32,512]{4,2,0,3,1:T(2,128)S(1)} collective-permute-done((f32[2,2,2,32,512]{4,2,0,3,1:T(2,128)S(1)}, f32[2,2,2,32,512]{4,2,0,3,1:T(2,128)S(1)}, u32[]{:S(2)}, u32[]{:S(2)}) %collective-permute-start.8) | collective-permute-done | bytes 524320 | tf_op jit(solution)/shard_map/ppermute | solution.py:20
  356.4 3.2 collective-permute-start.9
  371.2 6.2 dynamic_update_slice.12
  378.5 6.2 dynamic_update_slice.13
  385.8 6.1 dynamic_update_slice.14
  393.1 6.1 dynamic_update_slice.15
  399.2 6.1 copy.80
  405.4 8.6 %reshape.367 = f32[2048,256]{1,0:T(8,128)} reshape(f32[2048,2,4,32]{3,2,1,0:T(4,128)} %bitcast.197) | data formatting | bytes 4194304
  414.0 169.0 %all-reduce.2.cloned.1.call-done = f32[2,32,512]{2,1,0:T(8,128)} async-done(((f32[2,32,512]{2,1,0:T(8,128)}), f32[2,32,512]{2,1,0:T(8,128)}) %all-reduce.2.cloned.1.call-update) | async-done | bytes 131088 | tf_op jit(solution)/shard_map/psum | solution.py:175
  583.0 1.6 broadcast_multiply_fusion
  584.5 124.2 %reduce-scatter.4.cloned.1.call-done = f32[64,256]{1,0:T(8,128)} async-done(((f32[2048,256]{1,0:T(8,128)}), f32[64,256]{1,0:T(8,128)}) %reduce-scatter.4.cloned.1.call-update) | async-done | bytes 65552
  (123 shorter events, 46.3 us)
Async XLA Ops:
  7.2 78.2 %copy-start = (bf16[2,512,512]{2,1,0:T(8,128)(2,1)S(1)}, bf16[2,512,512]{2,1,0:T(8,128)(2,1)}, u32[]{:S(2)}) copy-start(bf16[2,512,512]{2,1,0:T(8,128)(2,1)} %param.6) | copy-start | bytes 3145732
  8.6 14.1 %copy-start.3 = (s32[64,2]{0,1:T(2,128)S(1)}, s32[64,2]{0,1:T(2,128)}, u32[]{:S(2)}) copy-start(s32[64,2]{0,1:T(2,128)} %param.7) | copy-start | bytes 1540
  8.6 14.2 %copy-start.6 = (s32[2]{0:T(128)S(1)}, s32[2]{0:T(128)}, u32[]{:S(2)}) copy-start(s32[2]{0:T(128)} %param.8) | copy-start | bytes 28
  8.6 15.0 %copy-start.4 = (s32[3]{0:T(128)S(1)}, s32[3]{0:T(128)}, u32[]{:S(2)}) copy-start(s32[3]{0:T(128)} %constant.136.clone.1) | copy-start | bytes 40
  10.9 40.3 %all-to-all-start = ((bf16[32,2,8192]{2,1,0:T(2,128)(2,1)}), bf16[32,2,8192]{2,1,0:T(2,128)(2,1)}, u32[]{:S(2)}, u32[]{:S(2)}) async-start(bf16[32,2,8192]{2,1,0:T(2,128)(2,1)} %reshape.371), calls=%async_computation | async-start | bytes 2097152 | tf_op jit(solution)/shard_map/all_to_all | solution.py:13
  70.2 9.9 %collective-permute-start = (bf16[2,2,2,32,512]{4,2,0,3,1:T(2,128)(2,1)S(1)}, bf16[2,2,2,32,512]{4,2,0,3,1:T(2,128)(2,1)S(1)}, u32[]{:S(2)}, u32[]{:S(2)}) collective-permute-start(bf16[2,2,2,32,512]{4,2,0,3,1:T(2,128)(2,1)S(1)} %pad_maximum_fusion.1), channel_id=1, source_target_pairs={{480,0},{0,32},{32,64},{64,96},{96,128},{128,160},{160,192},{192,2... | collective-permute-start | bytes 786440 | tf_op jit(solution)/shard_map/ppermute | solution.py:20
  80.5 13.9 %collective-permute-start.1 = (bf16[2,2,2,32,512]{4,2,0,3,1:T(2,128)(2,1)S(1)}, bf16[2,2,2,32,512]{4,2,0,3,1:T(2,128)(2,1)S(1)}, u32[]{:S(2)}, u32[]{:S(2)}) collective-permute-start(bf16[2,2,2,32,512]{4,2,0,3,1:T(2,128)(2,1)S(1)} %broadcast_select_fusion.4), channel_id=1, source_target_pairs={{448,0},{480,32},{0,64},{32,96},{64,128},{96,160},{128,192},{160,2... | collective-permute-start | bytes 786440 | tf_op jit(solution)/shard_map/ppermute | solution.py:20
  95.0 19.8 %collective-permute-start.2 = (bf16[2,2,2,32,512]{4,2,0,3,1:T(2,128)(2,1)S(1)}, bf16[2,2,2,32,512]{4,2,0,3,1:T(2,128)(2,1)S(1)}, u32[]{:S(2)}, u32[]{:S(2)}) collective-permute-start(bf16[2,2,2,32,512]{4,2,0,3,1:T(2,128)(2,1)S(1)} %broadcast_select_fusion.5), channel_id=1, source_target_pairs={{384,0},{416,32},{448,64},{480,96},{0,128},{32,160},{64,192},{96,2... | collective-permute-start | bytes 786440 | tf_op jit(solution)/shard_map/ppermute | solution.py:20
  115.1 10.1 %collective-permute-start.3 = (bf16[2,2,2,32,512]{4,2,0,3,1:T(2,128)(2,1)S(1)}, bf16[2,2,2,32,512]{4,2,0,3,1:T(2,128)(2,1)S(1)}, u32[]{:S(2)}, u32[]{:S(2)}) collective-permute-start(bf16[2,2,2,32,512]{4,2,0,3,1:T(2,128)(2,1)S(1)} %broadcast_select_fusion.6), channel_id=1, source_target_pairs={{256,0},{288,32},{320,64},{352,96},{384,128},{416,160},{448,192},{... | collective-permute-start | bytes 786440 | tf_op jit(solution)/shard_map/ppermute | solution.py:20
  125.7 13.5 %collective-permute-start.4 = (bf16[2,2,32,512]{3,1,0,2:T(2,128)(2,1)S(1)}, bf16[2,2,32,512]{3,1,0,2:T(2,128)(2,1)S(1)}, u32[]{:S(2)}, u32[]{:S(2)}) collective-permute-start(bf16[2,2,32,512]{3,1,0,2:T(2,128)(2,1)S(1)} %broadcast_select_fusion.8), channel_id=1, source_target_pairs={{32,0},{64,32},{96,64},{128,96},{160,128},{192,160},{224,192},{256... | collective-permute-start | bytes 393224 | tf_op jit(solution)/shard_map/ppermute | solution.py:20
  157.3 16.9 %all-to-all-start.1 = ((f32[16,1,2048]{2,1,0:T(1,128)}), f32[16,1,2048]{2,1,0:T(1,128)S(1)}, u32[]{:S(2)}, u32[]{:S(2)}) async-start(f32[16,1,2048]{2,1,0:T(1,128)} %reshape.373), calls=%async_computation.1 | async-start | bytes 262144 | tf_op jit(solution)/shard_map/all_to_all | solution.py:122
  174.2 19.2 %all-to-all-start.2 = ((f32[16,1,2048]{2,1,0:T(1,128)}), f32[16,1,2048]{2,1,0:T(1,128)S(1)}, u32[]{:S(2)}, u32[]{:S(2)}) async-start(f32[16,1,2048]{2,1,0:T(1,128)} %reshape.375), calls=%async_computation.2 | async-start | bytes 262144 | tf_op jit(solution)/shard_map/all_to_all | solution.py:123
  200.1 5.0 copy-start.5
  220.9 19.1 %all-to-all-start.3 = ((f32[16,1,2048]{2,1,0:T(1,128)}), f32[16,1,2048]{2,1,0:T(1,128)S(1)}, u32[]{:S(2)}, u32[]{:S(2)}) async-start(f32[16,1,2048]{2,1,0:T(1,128)} %reshape.379), calls=%async_computation.3 | async-start | bytes 262144 | tf_op jit(solution)/shard_map/all_to_all | solution.py:131
  240.1 15.8 %all-to-all-start.4 = ((f32[16,1,2048]{2,1,0:T(1,128)}), f32[16,1,2048]{2,1,0:T(1,128)S(1)}, u32[]{:S(2)}, u32[]{:S(2)}) async-start(f32[16,1,2048]{2,1,0:T(1,128)} %reshape.377), calls=%async_computation.4 | async-start | bytes 262144 | tf_op jit(solution)/shard_map/all_to_all | solution.py:132
  246.4 336.6 %all-reduce.2.cloned.1.call-start = ((), (), s32[]{:S(2)}) async-start(), calls=%async_computation.6 | async-start | bytes 262144 | tf_op jit(solution)/shard_map/psum | solution.py:175
  267.4 5.1 copy-start.2
  287.0 8.3 %collective-permute-start.5 = (f32[2,2,32,512]{3,1,0,2:T(2,128)S(1)}, f32[2,2,32,512]{3,1,0,2:T(2,128)S(1)}, u32[]{:S(2)}, u32[]{:S(2)}) collective-permute-start(f32[2,2,32,512]{3,1,0,2:T(2,128)S(1)} %slice.75), channel_id=1, source_target_pairs={{480,0},{0,32},{32,64},{64,96},{96,128},{128,160},{160,192},{192,2... | collective-permute-start | bytes 786440 | tf_op jit(solution)/shard_map/ppermute | solution.py:20
  295.8 13.3 %collective-permute-start.6 = (f32[2,2,2,32,512]{4,2,0,3,1:T(2,128)S(1)}, f32[2,2,2,32,512]{4,2,0,3,1:T(2,128)S(1)}, u32[]{:S(2)}, u32[]{:S(2)}) collective-permute-start(f32[2,2,2,32,512]{4,2,0,3,1:T(2,128)S(1)} %pad_maximum_fusion), channel_id=1, source_target_pairs={{480,0},{0,32},{32,64},{64,96},{96,128},{128,160},{160,192},{192,2... | collective-permute-start | bytes 1572872 | tf_op jit(solution)/shard_map/ppermute | solution.py:20
  309.5 24.0 %collective-permute-start.7 = (f32[2,2,2,32,512]{4,2,0,3,1:T(2,128)S(1)}, f32[2,2,2,32,512]{4,2,0,3,1:T(2,128)S(1)}, u32[]{:S(2)}, u32[]{:S(2)}) collective-permute-start(f32[2,2,2,32,512]{4,2,0,3,1:T(2,128)S(1)} %broadcast_select_fusion), channel_id=1, source_target_pairs={{448,0},{480,32},{0,64},{32,96},{64,128},{96,160},{128,192},{160,2... | collective-permute-start | bytes 1572872 | tf_op jit(solution)/shard_map/ppermute | solution.py:20
  334.0 22.1 %collective-permute-start.8 = (f32[2,2,2,32,512]{4,2,0,3,1:T(2,128)S(1)}, f32[2,2,2,32,512]{4,2,0,3,1:T(2,128)S(1)}, u32[]{:S(2)}, u32[]{:S(2)}) collective-permute-start(f32[2,2,2,32,512]{4,2,0,3,1:T(2,128)S(1)} %broadcast_select_fusion.1), channel_id=1, source_target_pairs={{384,0},{416,32},{448,64},{480,96},{0,128},{32,160},{64,192},{96,2... | collective-permute-start | bytes 1572872 | tf_op jit(solution)/shard_map/ppermute | solution.py:20
  356.4 12.6 %collective-permute-start.9 = (f32[2,2,2,32,512]{4,2,0,3,1:T(2,128)S(1)}, f32[2,2,2,32,512]{4,2,0,3,1:T(2,128)S(1)}, u32[]{:S(2)}, u32[]{:S(2)}) collective-permute-start(f32[2,2,2,32,512]{4,2,0,3,1:T(2,128)S(1)} %broadcast_select_fusion.2), channel_id=1, source_target_pairs={{256,0},{288,32},{320,64},{352,96},{384,128},{416,160},{448,192},{... | collective-permute-start | bytes 1572872 | tf_op jit(solution)/shard_map/ppermute | solution.py:20
  367.8 340.9 %reduce-scatter.4.cloned.1.call-start = ((), (), s32[]{:S(2)}) async-start(), calls=%async_computation.7 | async-start | bytes 2162688
  369.3 0.8 copy-start.1
Sparse Core Ops, SparseCore 0:
  368.0 214.9 all-reduce.1
  585.8 122.8 reduce-scatter.3
